TPU v7x, 32 devices: a whole 2x2x4 slice. The times are simulated.
32 devices in a mesh: section: 2 (over x), seq: 8 (over z, y), head: 2 (over core).
Axes of the slice: x: 2, y: 2, z: 4, core: 2. Of those that a mesh axis runs over, the one named last changes fastest.
Arguments:
- bwd_input: bfloat16 [2, 1024, 3584], P('section', 'seq', 'head'), may hold values from -6 to 6
- bwd_docs: int32 [2, 1024], P('section', 'seq'), may hold values from 0 to 3, as said below
- bwd_grad: bfloat16 [2, 1024, 3584], P('section', 'seq', 'head'), may hold values from -6 to 6
- proj_weight: bfloat16 [2, 256, 3584], P('section', 'seq', 'head'), may hold values from -0.09375 to 0.09375
- step_weight: float32 [2, 3584], P('section', 'head'), may hold values from -0.75 to 0.75
- step_bias: float32 [2, 56], P('section', 'head'), may hold values from -5 to -2
- rate_log: float32 [2, 56], P('section', 'head'), may hold values from -4 to 0.5
- skip_gain: float32 [2, 56], P('section', 'head'), may hold values from 0.5 to 1.5
Outputs:
- prev_grad: bfloat16 [2, 1024, 3584], P('section', 'seq', 'head')
- grad_proj: float32 [2, 256, 3584], P('section', 'seq', 'head')
- grad_step_weight: float32 [2, 3584], P('section', 'head')
- grad_step_bias: float32 [2, 56], P('section', 'head')
- grad_rate_log: float32 [2, 56], P('section', 'head')
- grad_skip: float32 [2, 56], P('section', 'head')
Inputs may be any that keep to these rules, and one draw needn't show every extreme that they name: `bwd_docs`: document ids of each row never fall, start at 0, every id occurs, and one document of each row holds 512 tokens.
All inputs are finite; a program needn't handle non-finite values.
Results may differ from a plain program's by a relative error of at most 0.023.
Values may be sent and summed in bfloat16 or wider, within the bound.
No kernel may reach another device: no remote copies, remote signals or barrier semaphores. Data moves between devices by JAX's collectives and lax.ppermute only.
A program may use at most 64 MiB of HBM per device.

v0:
```python
import jax
import jax.numpy as jnp
from jax import lax
from jax.sharding import PartitionSpec as P

EXACT = lax.Precision.HIGHEST


def shifted(block, axis, distance):
    devices = range(lax.axis_size(axis))
    route = [(i - distance, i) for i in devices if i - distance in devices]
    return lax.ppermute(block, axis, route)


def contract(spec, left, right):
    return jnp.einsum(spec, left, right, preferred_element_type=jnp.float32)


def local_setup(values, step_weight, step_bias, rate_log):
    tokens = values.shape[0]
    raw_step = (
        jnp.einsum("thp,hp->th", values.astype(jnp.float32), step_weight, precision=EXACT)
        + step_bias[None, :]
    )
    step_size = jax.nn.softplus(raw_step)
    decay_log = -jnp.exp(rate_log)[None, :] * step_size
    row_ids = lax.broadcasted_iota(jnp.int32, (tokens, tokens), 0)
    col_ids = lax.broadcasted_iota(jnp.int32, (tokens, tokens), 1)
    triangle = (row_ids >= col_ids).astype(jnp.float32)
    cumulative = jnp.dot(triangle, decay_log, precision=EXACT)
    return (step_size, cumulative, row_ids, col_ids)


def span_summary(values, mixer, step_weight, step_bias, rate_log, docs, doc_before):
    step_size, cumulative, row_ids, col_ids = local_setup(values, step_weight, step_bias, rate_log)
    final_log = cumulative[-1]
    tail_mask = (docs == docs[-1]).astype(jnp.float32)[:, None]
    tail_weight = (
        jnp.exp(jnp.where(tail_mask > 0, final_log[None, :] - cumulative, 0.0))
        * tail_mask
        * step_size
    )
    unbroken = (docs[-1] == doc_before).astype(jnp.float32)
    carry_decay = jnp.exp(final_log) * unbroken
    half_width = mixer.shape[1] // 2
    writers = mixer[:, :half_width]
    weighted = (tail_weight[:, :, None] * writers.astype(jnp.float32)[:, None, :]).astype(
        jnp.bfloat16
    )
    span_state = contract("thn,thp->hnp", weighted, values)
    return (carry_decay, span_state)


def span_output(
    values, mixer, step_weight, step_bias, rate_log, skip_gain, docs, doc_before, incoming
):
    step_size, cumulative, row_ids, col_ids = local_setup(values, step_weight, step_bias, rate_log)
    half_width = mixer.shape[1] // 2
    writers = mixer[:, :half_width]
    readers = mixer[:, half_width:]
    affinity = jnp.dot(readers, writers.T, preferred_element_type=jnp.float32)
    same_doc = ((docs[:, None] == docs[None, :]) & (row_ids >= col_ids)).astype(jnp.float32)
    heads_first = cumulative.T
    log_gap = heads_first[:, :, None] - heads_first[:, None, :]
    mixing = (
        jnp.exp(jnp.where(same_doc[None] > 0, log_gap, 0.0))
        * same_doc[None]
        * affinity[None]
        * step_size.T[:, None, :]
    )
    mixing = mixing.astype(jnp.bfloat16)
    local_part = contract("hts,shp->thp", mixing, values)
    unbroken = (docs == doc_before).astype(jnp.float32)
    carry_scale = jnp.exp(cumulative) * unbroken[:, None]
    carried = jnp.einsum("tn,hnp->thp", readers.astype(jnp.float32), incoming, precision=EXACT)
    combined = (
        values.astype(jnp.float32) * (1.0 + skip_gain)[None, :, None]
        + local_part
        + carry_scale[:, :, None] * carried
    )
    return combined.astype(jnp.bfloat16)


def scan_rounds(decay, state, axis, forward):
    size, mine = (lax.axis_size(axis), lax.axis_index(axis))
    far_decay, far_state = (decay, state)
    near_decay = jnp.ones_like(decay)
    near_state = jnp.zeros_like(state)
    distance = 1
    while distance < size:
        got_decay, got_state = shifted(
            (far_decay, far_state.astype(jnp.bfloat16)), axis, distance if forward else -distance
        )
        got_state = got_state.astype(jnp.float32)
        near_state = near_state + near_decay[:, None] * got_state
        near_decay = near_decay * got_decay
        if distance * 2 < size:
            far_state = far_state + far_decay[:, None] * got_state
            far_decay = far_decay * got_decay
        distance *= 2
    return near_state


def shards(bwd_input, bwd_docs, bwd_grad, proj_weight, step_weight, step_bias, rate_log, skip_gain):
    tokens = bwd_input.shape[1]
    channels_here = bwd_input.shape[2]
    heads_here = step_bias.shape[1]
    head_width = channels_here // heads_here
    bwd_flat = bwd_input[0]
    bwd_values = bwd_flat.reshape(tokens, heads_here, head_width)
    weight_heads = step_weight[0].reshape(heads_here, head_width)
    bias_heads = step_bias[0]
    rate_heads = rate_log[0]
    skip_heads = skip_gain[0]
    docs_bwd = bwd_docs[0]
    doc_before = shifted(docs_bwd[-1:], "seq", 1)[0]
    full_weight = lax.all_gather(proj_weight[0], "seq", axis=0, tiled=True)
    partial_value = jnp.dot(bwd_flat, full_weight.T, preferred_element_type=jnp.float32)
    mixer_bwd = lax.psum_scatter(
        partial_value.astype(jnp.bfloat16), "head", scatter_dimension=1, tiled=True
    )
    cotangent = bwd_grad[0].reshape(tokens, heads_here, head_width)

    def summary_bwd(values_in, mixer_in, weight_in, bias_in, rate_in):
        return span_summary(values_in, mixer_in, weight_in, bias_in, rate_in, docs_bwd, doc_before)

    summary_out, summary_pull = jax.vjp(
        summary_bwd, bwd_values, mixer_bwd, weight_heads, bias_heads, rate_heads
    )
    decay_bwd, state_bwd = summary_out
    state_shape = state_bwd.shape
    state_flat = state_bwd.reshape(heads_here, -1)

    def output_bwd(values_in, mixer_in, weight_in, bias_in, rate_in, skip_in, state_in):
        return span_output(
            values_in,
            mixer_in,
            weight_in,
            bias_in,
            rate_in,
            skip_in,
            docs_bwd,
            doc_before,
            state_in,
        )

    def carried_only(state_in):
        return output_bwd(
            bwd_values, mixer_bwd, weight_heads, bias_heads, rate_heads, skip_heads, state_in
        )

    state_grad = jax.vjp(carried_only, jnp.zeros(state_shape, jnp.float32))[1](cotangent)[0]
    state_grad = state_grad.reshape(heads_here, -1)
    incoming_flat = scan_rounds(decay_bwd, state_flat, "seq", True)
    adjoint_flat = scan_rounds(decay_bwd, state_grad, "seq", False)
    incoming_bwd = incoming_flat.reshape(state_shape)
    unused, output_pull = jax.vjp(
        output_bwd,
        bwd_values,
        mixer_bwd,
        weight_heads,
        bias_heads,
        rate_heads,
        skip_heads,
        incoming_bwd,
    )
    out_grads = output_pull(cotangent)
    decay_grad = jnp.sum(adjoint_flat * incoming_flat, axis=1)
    sum_grads = summary_pull((decay_grad, adjoint_flat.reshape(state_shape)))
    mixer_grad = (out_grads[1].astype(jnp.float32) + sum_grads[1].astype(jnp.float32)).astype(
        jnp.bfloat16
    )
    mixer_full = lax.all_gather(mixer_grad, "head", axis=1, tiled=True)
    back_proj = jnp.dot(mixer_full, full_weight, preferred_element_type=jnp.float32)
    value_grad = (out_grads[0].astype(jnp.float32) + sum_grads[0].astype(jnp.float32)).reshape(
        tokens, channels_here
    ) + back_proj
    value_grad = value_grad.astype(jnp.bfloat16)
    prev_part = shifted(value_grad.reshape(1, tokens, channels_here), "section", -1)
    grad_rows = lax.psum_scatter(
        lax.dot_general(
            mixer_full, bwd_flat, (((0,), (0,)), ((), ())), preferred_element_type=jnp.float32
        ).astype(jnp.bfloat16),
        "seq",
        scatter_dimension=0,
        tiled=True,
    ).astype(jnp.float32)
    totals = lax.psum(
        (
            (out_grads[2] + sum_grads[2]).reshape(channels_here),
            out_grads[3] + sum_grads[3],
            out_grads[4] + sum_grads[4],
            out_grads[5],
        ),
        "seq",
    )
    return (
        prev_part,
        grad_rows[None],
        totals[0][None],
        totals[1][None],
        totals[2][None],
        totals[3][None],
    )


def solution(mesh):
    in_specs = (
        P("section", "seq", "head"),
        P("section", "seq"),
        P("section", "seq", "head"),
        P("section", "seq", "head"),
        P("section", "head"),
        P("section", "head"),
        P("section", "head"),
        P("section", "head"),
    )
    out_specs = (
        P("section", "seq", "head"),
        P("section", "seq", "head"),
        P("section", "head"),
        P("section", "head"),
        P("section", "head"),
        P("section", "head"),
    )
    return jax.shard_map(shards, mesh=mesh, in_specs=in_specs, out_specs=out_specs, check_vma=False)
```

profile of v0, /device:TPU:0, one launch (start us, length us, event | category | flops | bytes accessed | tf_op | source)
XLA Modules:
  0.0 210.8 jit_solution(10798965876663877636)
XLA Ops:
  8.5 5.4 %collective-permute-start.1 = (s32[1]{0:T(128)}, s32[1]{0:T(128)}, u32[]{:S(2)}, u32[]{:S(2)}) collective-permute-start(s32[1]{0:T(128)} %bitcast.18), channel_id=1, source_target_pairs={{0,2},{2,4},{4,6},{6,8},{8,10},{10,12},{12,14},{1,3},{3,5},{5,7},{... | collective-permute-start | bytes 20 | tf_op jit(solution)/shard_map/ppermute | solution.py:12
  13.9 32.6 %all-gather = bf16[1,256,1792]{2,1,0:T(8,128)(2,1)S(1)} all-gather(bf16[1,32,1792]{2,1,0:T(8,128)(2,1)} %param.12), channel_id=2, replica_groups=mesh['section'=2,'seq'=8,'head'=2] {'seq'}, dimensions={1}, use_global_device_ids=true | all-gather | bytes 1032192 | tf_op jit(solution)/shard_map/all_gather | solution.py:117
  54.9 1.4 fusion.37
  56.2 1.5 reshape.210
  58.5 4.3 %collective-permute-start = (bf16[28,4096]{1,0:T(8,128)(2,1)}, bf16[28,4096]{1,0:T(8,128)(2,1)}, u32[]{:S(2)}, u32[]{:S(2)}) collective-permute-start(bf16[28,4096]{1,0:T(8,128)(2,1)} %convert_element_type.189), channel_id=1, source_target_pairs={{0,2},{2,4},{4,6},{6,8},{8,10},{10,12},{12,14},{1,3},{3,5},{5,7},{... | collective-permute-start | bytes 688136 | tf_op jit(solution)/shard_map/ppermute | solution.py:12
  62.8 1.6 convolution_bitcast_fusion
  64.4 2.4 %copy.93 = f32[28,64,64]{2,1,0:T(8,128)} copy(f32[28,64,64]{1,2,0:T(8,128)} %convolution_bitcast_fusion) | data formatting | bytes 917504 | tf_op jit(solution)/shard_map/transpose(jvp(tn,hnp->thp))/transpose | solution.py:75
  66.8 1.5 reshape.212
  68.3 1.3 collective-permute-start.6
  70.7 4.8 %collective-permute-start.3 = (bf16[28,4096]{1,0:T(8,128)(2,1)S(1)}, bf16[28,4096]{1,0:T(8,128)(2,1)S(1)}, u32[]{:S(2)}, u32[]{:S(2)}) collective-permute-start(bf16[28,4096]{1,0:T(8,128)(2,1)S(1)} %fusion.56), channel_id=1, source_target_pairs={{0,4},{2,6},{4,8},{6,10},{8,12},{10,14},{1,5},{3,7},{5,9},{7,11},{... | collective-permute-start | bytes 688136 | tf_op jit(solution)/shard_map/ppermute | solution.py:12
  75.6 2.5 %collective-permute-start.2 = (f32[28]{0:T(128)S(1)}, f32[28]{0:T(128)S(1)}, u32[]{:S(2)}, u32[]{:S(2)}) collective-permute-start(f32[28]{0:T(128)S(1)} %copy-done.36), channel_id=1, source_target_pairs={{0,2},{2,4},{4,6},{6,8},{8,10},{10,12},{12,14},{1,3},{3,5},{5,7},{... | collective-permute-start | bytes 344 | tf_op jit(solution)/shard_map/ppermute | solution.py:12
  79.4 4.5 %collective-permute-done.7 = f32[28]{0:T(128)S(1)} collective-permute-done((f32[28]{0:T(128)S(1)}, f32[28]{0:T(128)S(1)}, u32[]{:S(2)}, u32[]{:S(2)}) %collective-permute-start.7) | collective-permute-done | bytes 144 | tf_op jit(solution)/shard_map/ppermute | solution.py:12
  84.3 2.0 fusion.41
  86.4 1.4 collective-permute-start.8
  88.5 5.5 %collective-permute-start.5 = (bf16[28,4096]{1,0:T(8,128)(2,1)}, bf16[28,4096]{1,0:T(8,128)(2,1)S(1)}, u32[]{:S(2)}, u32[]{:S(2)}) collective-permute-start(bf16[28,4096]{1,0:T(8,128)(2,1)} %get-tuple-element.40), channel_id=1, source_target_pairs={{0,8},{2,10},{4,12},{6,14},{1,9},{3,11},{5,13},{7,15},{16,24},{18,... | collective-permute-start | bytes 688136 | tf_op jit(solution)/shard_map/ppermute | solution.py:12
  97.7 1.4 reshape_squeeze.10
  99.1 2.6 %fusion.25 = (f32[1792]{0:T(1024)}, f32[1,128,1792]{1,2,0:T(8,128)}) fusion(bf16[1,128,1792]{1,2,0:T(8,128)(2,1)S(1)} %copy.81, bf16[1,128,1792]{1,2,0:T(8,128)(2,1)S(1)} %copy.82, f32[128,28]{0,1:T(8,128)} %copy-done.12), kind=kLoop, calls=%fused_computation.45 | loop fusion | flops 1145088 | bytes 1856512 | tf_op jit(solution)/shard_map/transpose(jvp())/reduce_sum | solution.py:77
  101.6 1.4 reduce_sum.160
  103.0 4.0 %collective-permute-start.4 = (f32[28]{0:T(128)}, f32[28]{0:T(128)}, u32[]{:S(2)}, u32[]{:S(2)}) collective-permute-start(f32[28]{0:T(128)} %copy-done.49), channel_id=1, source_target_pairs={{0,4},{2,6},{4,8},{6,10},{8,12},{10,14},{1,5},{3,7},{5,9},{7,11},{... | collective-permute-start | bytes 344 | tf_op jit(solution)/shard_map/ppermute | solution.py:12
  107.0 1.4 reduce_sum.161
  110.3 4.3 %collective-permute-done.9 = f32[28]{0:T(128)S(1)} collective-permute-done((f32[28]{0:T(128)}, f32[28]{0:T(128)S(1)}, u32[]{:S(2)}, u32[]{:S(2)}) %collective-permute-start.9) | collective-permute-done | bytes 144 | tf_op jit(solution)/shard_map/ppermute | solution.py:12
  116.8 2.9 %multiply_reduce_fusion.2 = (f32[28]{0:T(128)}, bf16[28,4096]{1,0:T(8,128)(2,1)S(1)}, f32[28,4096]{1,0:T(8,128)}) fusion(bf16[28,4096]{1,0:T(8,128)(2,1)} %collective-permute-done.10, f32[28]{0:T(128)S(1)} %mul.365, bf16[28,4096]{1,0:T(8,128)(2,1)S(1)} %collective-permute-done.8, f32[28]{0:T(128)} %copy-done.46, bf16[28,4096]{1,0:T(8,128)(2,1)S(1)} %copy-done.2, ...), kind=kLoop, calls=%fused_computation.79 | loop fusion | flops 1949668 | bytes 2064944 | tf_op jit(solution)/shard_map/reduce_sum | solution.py:168
  122.4 2.5 %fusion.12 = (f32[28,128]{1,0:T(8,128)}, f32[28,128]{1,0:T(8,128)}, f32[28,128]{1,0:T(8,128)S(1)}, bf16[128,128]{1,0:T(8,128)(2,1)S(1)}) fusion(f32[28,128]{1,0:T(8,128)S(1)} %copy.85, f32[128,128]{1,0:T(8,128)S(1)} %copy-done.15, f32[128,128]{1,0:T(8,128)S(1)} %copy-done.17, f32[28,128]{1,0:T(8,128)S(1)} %bitcast.243, pred[128,128]{1,0:T(8,128)(4,1)S(1)} %copy-done.25, ...), kind=kOutput, calls=%fused_computation.19 | convolution fusion | flops 66491904 | bytes 1169408 | tf_op jit(solution)/shard_map/transpose(jvp(hts,shp->thp))/dot_general | solution.py:16
  125.2 1.4 reshape.211
  127.8 1.7 fusion.87
  131.1 2.2 %fusion.24 = bf16[128,64]{0,1:T(8,128)(2,1)S(1)} fusion(bf16[128,64]{0,1:T(8,128)(2,1)S(1)} %convolution_convert_fusion.7, f32[128,28,64]{0,2,1:T(8,128)} %bitcast.228, f32[28,64,64]{2,1,0:T(8,128)S(1)} %reshape.211), kind=kOutput, calls=%fused_computation.44 | convolution fusion | flops 176177152 | bytes 1409024 | tf_op jit(solution)/shard_map/transpose(jvp(tn,hnp->thp))/dot_general | solution.py:75
  133.2 2.0 all_gather.7
  135.4 1.4 convolution_convert_fusion
  140.6 1.4 collective-permute-start.11
  143.9 22.8 %all-reduce.4 = (f32[1,1792]{1,0:T(1,128)}, f32[1,28]{1,0:T(1,128)}, f32[1,28]{1,0:T(1,128)}, f32[1,28]{1,0:T(1,128)}) all-reduce(f32[1,1792]{1,0:T(1,128)S(1)} %broadcast_in_dim.47, f32[1,28]{1,0:T(1,128)S(1)} %get-tuple-element.50, f32[1,28]{1,0:T(1,128)S(1)} %get-tuple-element.49, ...), channel_id=1, replica_groups=mesh['section'=2,'seq'=8,'head'=2] {'seq'}, use_global_device_ids=true, to_apply=%region_11.13 | all-reduce | flops 1876 | bytes 15008 | tf_op jit(solution)/shard_map/psum | solution.py:188
  166.7 34.9 %reduce-scatter.5.cloned.1.call-done = bf16[32,1792]{1,0:T(8,128)(2,1)} async-done(((bf16[256,1792]{1,0:T(8,128)(2,1)}), bf16[32,1792]{1,0:T(8,128)(2,1)}) %reduce-scatter.5.cloned.1.call-update) | async-done | bytes 114704 | tf_op jit(solution)/shard_map/reduce_scatter | solution.py:180
  201.6 1.6 bitcast_convert_fusion
  (202 shorter events, 32.0 us)
Async XLA Ops:
  7.2 39.4 %copy-start = (bf16[1,128,1792]{2,1,0:T(8,128)(2,1)S(1)}, bf16[1,128,1792]{2,1,0:T(8,128)(2,1)}, u32[]{:S(2)}) copy-start(bf16[1,128,1792]{2,1,0:T(8,128)(2,1)} %param.9) | copy-start | bytes 1376260
  7.2 47.0 %reduce-scatter.7.cloned.1.call-start = ((), (), s32[]{:S(2)}) async-start(), calls=%async_computation.3 | async-start | bytes 98304
  8.5 40.6 %collective-permute-start.1 = (s32[1]{0:T(128)}, s32[1]{0:T(128)}, u32[]{:S(2)}, u32[]{:S(2)}) collective-permute-start(s32[1]{0:T(128)} %bitcast.18), channel_id=1, source_target_pairs={{0,2},{2,4},{4,6},{6,8},{8,10},{10,12},{12,14},{1,3},{3,5},{5,7},{... | collective-permute-start | bytes 20 | tf_op jit(solution)/shard_map/ppermute | solution.py:12
  47.8 153.8 %reduce-scatter.5.cloned.1.call-start = ((), (), s32[]{:S(2)}) async-start(), calls=%async_computation.2 | async-start | bytes 1032192 | tf_op jit(solution)/shard_map/reduce_scatter | solution.py:180
  48.1 3.6 %copy-start.37 = (f32[1,28]{1,0:T(1,128)S(1)}, f32[1,28]{1,0:T(1,128)}, u32[]{:S(2)}) copy-start(f32[1,28]{1,0:T(1,128)} %param.14) | copy-start | bytes 340
  48.9 7.3 %copy-start.59 = (f32[28]{0:T(128)}, f32[28]{0:T(128)S(1)}, u32[]{:S(2)}) copy-start(f32[28]{0:T(128)S(1)} %negate_bitcast_fusion) | copy-start | bytes 340
  50.5 5.8 %copy-start.28 = (pred[128]{0:T(512)(128)(4,1)}, pred[128]{0:T(512)(128)(4,1)S(1)}, u32[]{:S(2)}) copy-start(pred[128]{0:T(512)(128)(4,1)S(1)} %get-tuple-element.31) | copy-start | bytes 388
  50.5 5.7 %copy-start.31 = (f32[128]{0:T(128)}, f32[128]{0:T(128)S(1)}, u32[]{:S(2)}) copy-start(f32[128]{0:T(128)S(1)} %get-tuple-element.32) | copy-start | bytes 1540
  52.0 10.8 %copy-start.12 = (f32[128,28]{0,1:T(8,128)}, f32[128,28]{0,1:T(8,128)S(1)}, u32[]{:S(2)}) copy-start(f32[128,28]{0,1:T(8,128)S(1)} %get-tuple-element.47) | copy-start | bytes 43012
  52.2 5.6 %copy-start.40 = (f32[28]{0:T(128)}, f32[28]{0:T(128)S(1)}, u32[]{:S(2)}) copy-start(f32[28]{0:T(128)S(1)} %slice_bitcast_fusion) | copy-start | bytes 340
  56.2 6.6 %copy-start.8 = (bf16[128,128]{1,0:T(8,128)(2,1)S(1)}, bf16[128,128]{1,0:T(8,128)(2,1)}, u32[]{:S(2)}) copy-start(bf16[128,128]{1,0:T(8,128)(2,1)} %reduce-scatter.7.cloned.1.call-done) | copy-start | bytes 98308
  58.5 11.2 %collective-permute-start = (bf16[28,4096]{1,0:T(8,128)(2,1)}, bf16[28,4096]{1,0:T(8,128)(2,1)}, u32[]{:S(2)}, u32[]{:S(2)}) collective-permute-start(bf16[28,4096]{1,0:T(8,128)(2,1)} %convert_element_type.189), channel_id=1, source_target_pairs={{0,2},{2,4},{4,6},{6,8},{8,10},{10,12},{12,14},{1,3},{3,5},{5,7},{... | collective-permute-start | bytes 688136 | tf_op jit(solution)/shard_map/ppermute | solution.py:12
  68.3 7.3 %copy-start.36 = (f32[28]{0:T(128)S(1)}, f32[28]{0:T(128)}, u32[]{:S(2)}) copy-start(f32[28]{0:T(128)} %exponential_multiply_fusion.1) | copy-start | bytes 340
  68.3 15.5 %collective-permute-start.6 = (bf16[28,4096]{1,0:T(8,128)(2,1)S(1)}, bf16[28,4096]{1,0:T(8,128)(2,1)S(1)}, u32[]{:S(2)}, u32[]{:S(2)}) collective-permute-start(bf16[28,4096]{1,0:T(8,128)(2,1)S(1)} %convert_element_type.200), channel_id=1, source_target_pairs={{2,0},{4,2},{6,4},{8,6},{10,8},{12,10},{14,12},{3,1},{5,3},{7,5},{... | collective-permute-start | bytes 688136 | tf_op jit(solution)/shard_map/ppermute | solution.py:12
  70.7 13.2 %collective-permute-start.3 = (bf16[28,4096]{1,0:T(8,128)(2,1)S(1)}, bf16[28,4096]{1,0:T(8,128)(2,1)S(1)}, u32[]{:S(2)}, u32[]{:S(2)}) collective-permute-start(bf16[28,4096]{1,0:T(8,128)(2,1)S(1)} %fusion.56), channel_id=1, source_target_pairs={{0,4},{2,6},{4,8},{6,10},{8,12},{10,14},{1,5},{3,7},{5,9},{7,11},{... | collective-permute-start | bytes 688136 | tf_op jit(solution)/shard_map/ppermute | solution.py:12
  75.6 3.8 %collective-permute-start.2 = (f32[28]{0:T(128)S(1)}, f32[28]{0:T(128)S(1)}, u32[]{:S(2)}, u32[]{:S(2)}) collective-permute-start(f32[28]{0:T(128)S(1)} %copy-done.36), channel_id=1, source_target_pairs={{0,2},{2,4},{4,6},{6,8},{8,10},{10,12},{12,14},{1,3},{3,5},{5,7},{... | collective-permute-start | bytes 344 | tf_op jit(solution)/shard_map/ppermute | solution.py:12
  78.0 5.8 %collective-permute-start.7 = (f32[28]{0:T(128)S(1)}, f32[28]{0:T(128)S(1)}, u32[]{:S(2)}, u32[]{:S(2)}) collective-permute-start(f32[28]{0:T(128)S(1)} %copy-done.36), channel_id=1, source_target_pairs={{2,0},{4,2},{6,4},{8,6},{10,8},{12,10},{14,12},{3,1},{5,3},{7,5},{... | collective-permute-start | bytes 344 | tf_op jit(solution)/shard_map/ppermute | solution.py:12
  79.4 4.5 %copy-start.45 = (f32[28]{0:T(128)}, f32[28]{0:T(128)S(1)}, u32[]{:S(2)}) copy-start(f32[28]{0:T(128)S(1)} %collective-permute-done.2) | copy-start | bytes 340
  83.9 11.1 %copy-start.47 = (f32[28]{0:T(128)}, f32[28]{0:T(128)S(1)}, u32[]{:S(2)}) copy-start(f32[28]{0:T(128)S(1)} %get-tuple-element.43) | copy-start | bytes 340
  83.9 11.0 %copy-start.1 = (bf16[28,4096]{1,0:T(8,128)(2,1)}, bf16[28,4096]{1,0:T(8,128)(2,1)S(1)}, u32[]{:S(2)}) copy-start(bf16[28,4096]{1,0:T(8,128)(2,1)S(1)} %collective-permute-done.6) | copy-start | bytes 688132
  84.3 3.4 %copy-start.35 = (s32[1,128]{1,0:T(1,128)S(1)}, s32[1,128]{1,0:T(1,128)}, u32[]{:S(2)}) copy-start(s32[1,128]{1,0:T(1,128)} %param.10) | copy-start | bytes 1540
  86.4 10.7 %copy-start.58 = (f32[1,28]{1,0:T(1,128)S(1)}, f32[1,28]{1,0:T(1,128)}, u32[]{:S(2)}) copy-start(f32[1,28]{1,0:T(1,128)} %param.16) | copy-start | bytes 340
  86.4 8.6 %collective-permute-start.8 = (bf16[28,4096]{1,0:T(8,128)(2,1)S(1)}, bf16[28,4096]{1,0:T(8,128)(2,1)S(1)}, u32[]{:S(2)}, u32[]{:S(2)}) collective-permute-start(bf16[28,4096]{1,0:T(8,128)(2,1)S(1)} %get-tuple-element.41), channel_id=1, source_target_pairs={{4,0},{6,2},{8,4},{10,6},{12,8},{14,10},{5,1},{7,3},{9,5},{11,7},{... | collective-permute-start | bytes 688136 | tf_op jit(solution)/shard_map/ppermute | solution.py:12
  88.5 27.6 %collective-permute-start.5 = (bf16[28,4096]{1,0:T(8,128)(2,1)}, bf16[28,4096]{1,0:T(8,128)(2,1)S(1)}, u32[]{:S(2)}, u32[]{:S(2)}) collective-permute-start(bf16[28,4096]{1,0:T(8,128)(2,1)} %get-tuple-element.40), channel_id=1, source_target_pairs={{0,8},{2,10},{4,12},{6,14},{1,9},{3,11},{5,13},{7,15},{16,24},{18,... | collective-permute-start | bytes 688136 | tf_op jit(solution)/shard_map/ppermute | solution.py:12
  95.8 21.0 %collective-permute-start.10 = (bf16[28,4096]{1,0:T(8,128)(2,1)}, bf16[28,4096]{1,0:T(8,128)(2,1)}, u32[]{:S(2)}, u32[]{:S(2)}) collective-permute-start(bf16[28,4096]{1,0:T(8,128)(2,1)} %fusion.45), channel_id=1, source_target_pairs={{8,0},{10,2},{12,4},{14,6},{9,1},{11,3},{13,5},{15,7},{24,16},{26,... | collective-permute-start | bytes 688136 | tf_op jit(solution)/shard_map/ppermute | solution.py:12
  99.0 17.8 %copy-start.2 = (bf16[28,4096]{1,0:T(8,128)(2,1)S(1)}, bf16[28,4096]{1,0:T(8,128)(2,1)}, u32[]{:S(2)}) copy-start(bf16[28,4096]{1,0:T(8,128)(2,1)} %copy-done.1) | copy-start | bytes 688132
  99.1 17.8 %copy-start.6 = (bf16[28,4096]{1,0:T(8,128)(2,1)S(1)}, bf16[28,4096]{1,0:T(8,128)(2,1)}, u32[]{:S(2)}) copy-start(bf16[28,4096]{1,0:T(8,128)(2,1)} %copy-done.5) | copy-start | bytes 688132
  103.0 6.6 %collective-permute-start.4 = (f32[28]{0:T(128)}, f32[28]{0:T(128)}, u32[]{:S(2)}, u32[]{:S(2)}) collective-permute-start(f32[28]{0:T(128)} %copy-done.49), channel_id=1, source_target_pairs={{0,4},{2,6},{4,8},{6,10},{8,12},{10,14},{1,5},{3,7},{5,9},{7,11},{... | collective-permute-start | bytes 344 | tf_op jit(solution)/shard_map/ppermute | solution.py:12
  108.3 6.3 %collective-permute-start.9 = (f32[28]{0:T(128)}, f32[28]{0:T(128)S(1)}, u32[]{:S(2)}, u32[]{:S(2)}) collective-permute-start(f32[28]{0:T(128)} %copy-done.47), channel_id=1, source_target_pairs={{4,0},{6,2},{8,4},{10,6},{12,8},{14,10},{5,1},{7,3},{9,5},{11,7},{... | collective-permute-start | bytes 344 | tf_op jit(solution)/shard_map/ppermute | solution.py:12
  140.5 3.2 %copy-start.51 = (f32[1,28]{1,0:T(1,128)S(1)}, f32[1,28]{1,0:T(1,128)}, u32[]{:S(2)}) copy-start(f32[1,28]{1,0:T(1,128)} %param.15) | copy-start | bytes 340
  140.6 3.2 %copy-start.48 = (f32[28]{0:T(128)S(1)}, f32[28]{0:T(128)}, u32[]{:S(2)}) copy-start(f32[28]{0:T(128)} %reduce_sum.161) | copy-start | bytes 340
  140.6 26.1 %collective-permute-start.11 = (bf16[1,128,1792]{2,1,0:T(8,128)(2,1)S(1)}, bf16[1,128,1792]{2,1,0:T(8,128)(2,1)S(1)}, u32[]{:S(2)}, u32[]{:S(2)}) collective-permute-start(bf16[1,128,1792]{2,1,0:T(8,128)(2,1)S(1)} %fusion.1), channel_id=1, source_target_pairs={{16,0},{17,1},{18,2},{19,3},{20,4},{21,5},{22,6},{23,7},{24,8},{25... | collective-permute-start | bytes 1376264 | tf_op jit(solution)/shard_map/ppermute | solution.py:12
  (46 other events, 79.0 us)
Sparse Core Ops, SparseCore 0:
  47.9 6.1 reduce-scatter.6
  136.9 64.6 reduce-scatter.4
where the time goes:
time: 212 us; the launch traced here: 211 us
  blocking collectives  57.5 us (27%)
  waiting for transfers between devices  45.5 us (21%)
  starting transfers between devices  34.5 us (16%)
  other arithmetic  20.5 us (10%)
  local copies, waits for them, and re-layouts  18.9 us (9%)
  matrix products  17.6 us (8%)
  between operations  16.3 us (8%)
    reduce_scatter x1, waiting for transfers between devices, shards(): lax.psum_scatter(lax.dot_general(mixer_full, bwd_flat, (((0,), (0,)), (()...  34.9 us
    ppermute x12, starting transfers between devices, shifted(): return lax.ppermute(block, axis, route)  34.4 us
    all_gather x1, blocking collectives, shards(): full_weight = lax.all_gather(proj_weight[0], 'seq', axis=0, tiled=True)  32.6 us
    psum x1, blocking collectives, shards(): lax.psum(((out_grads[2] + sum_grads[2]).reshape(channels_here), out_grads...  22.8 us
    ppermute x12, waiting for transfers between devices, shifted(): return lax.ppermute(block, axis, route)  9.77 us
    dot_general x5, matrix products, contract(): return jnp.einsum(spec, left, right, preferred_element_type=jnp.float32)  5.53 us
    convert_element_type x5, other arithmetic, scan_rounds(): far_state.astype(jnp.bfloat16)  4.74 us
    unnamed x132, local copies, waits for them, and re-layouts  4.31 us
  transfers between devices with their start and end apart: 14, of which 5 were waited for; matrix products, arithmetic and copies ran while one was open for 13% of the time, Pallas kernels for 0%

commit v1 on v0

--- a/solution.py
+++ b/solution.py
@@ -114,7 +114,22 @@
     skip_heads = skip_gain[0]
     docs_bwd = bwd_docs[0]
     doc_before = shifted(docs_bwd[-1:], "seq", 1)[0]
-    full_weight = lax.all_gather(proj_weight[0], "seq", axis=0, tiled=True)
+
+    def assign_streams(tile_in):
+        chip_axis = "seq"
+        parts_n = jax.lax.axis_size(chip_axis)
+        crops = [(dd, (dd + 1) % parts_n) for dd in range(parts_n)]
+        entries = [(dd, (dd - 1) % parts_n) for dd in range(parts_n)]
+        v_now, y = ([tile_in], [tile_in])
+        for _ in range(parts_n // 2):
+            v_now.append(jax.lax.ppermute(v_now[-1], chip_axis, perm=crops))
+        for _ in range((parts_n - 1) // 2):
+            y.append(jax.lax.ppermute(y[-1], chip_axis, perm=entries))
+        now = jnp.concatenate([*v_now[::-1], *y[1:]], axis=0)
+        carry = jax.lax.axis_index(chip_axis)
+        return jnp.roll(now, (carry - parts_n // 2) * tile_in.shape[0], axis=0)
+
+    full_weight = assign_streams(proj_weight[0])
     partial_value = jnp.dot(bwd_flat, full_weight.T, preferred_element_type=jnp.float32)
     mixer_bwd = lax.psum_scatter(
         partial_value.astype(jnp.bfloat16), "head", scatter_dimension=1, tiled=True

time: 212 us -> 211 us (level)
  blocking collectives: 57.5 us -> 23 us
  starting transfers between devices: 34.5 us -> 52.3 us
  waiting for transfers between devices: 45.5 us -> 57.6 us
  local copies, waits for them, and re-layouts: 18.9 us -> 23.7 us
  other arithmetic: 20.5 us -> 17.2 us
  matrix products: 17.6 us -> 20.4 us
    all_gather x1 -> x0, blocking collectives: 32.6 us -> none  [shards(): full_weight = lax.all_gather(proj_weight[0], 'seq', axis=0, tiled=True)]
    ppermute x0 -> x7, starting transfers between devices: none -> 17.1 us  [the longest x3 12.6 us: assign_streams(): y.append(jax.lax.ppermute(y[-1], chip_axis, perm=entries))]
    ppermute x0 -> x7, waiting for transfers between devices: none -> 9.68 us  [the longest x4 9.68 us: assign_streams(): v_now.append(jax.lax.ppermute(v_now[-1], chip_axis, perm=crops))]
    unnamed x132 -> x104, local copies, waits for them, and re-layouts: 4.31 us -> 12.4 us
    reduce_scatter x0 -> x1, waiting for transfers between devices: none -> 5.95 us  [shards(): lax.psum_scatter(partial_value.astype(jnp.bfloat16), 'head', scatter_dime...]
    reduce_sum x2, other arithmetic: 3.95 us -> 0.97 us  [span_output(): values.astype(jnp.float32) * (1.0 + skip_gain)[None, :, None] + local_part]
    ppermute x12, waiting for transfers between devices: 9.77 us -> 7.62 us  [shifted(): return lax.ppermute(block, axis, route)]
  transfers between devices with their start and end apart: 14 -> 21, of which waited for: 5 -> 8; matrix products, arithmetic and copies ran while one was open for 13% -> 12% of each run, Pallas kernels for 0% -> 0%
where the time goes in v1:
time: 211 us; the launch traced here: 210 us
  waiting for transfers between devices  57.6 us (27%)
  starting transfers between devices  52.3 us (25%)
  local copies, waits for them, and re-layouts  23.7 us (11%)
  blocking collectives  23 us (11%)
  matrix products  20.4 us (10%)
  other arithmetic  17.2 us (8%)
  between operations  16.1 us (8%)
    ppermute x12, starting transfers between devices, shifted(): return lax.ppermute(block, axis, route)  35.1 us
    reduce_scatter x1, waiting for transfers between devices, shards(): lax.psum_scatter(lax.dot_general(mixer_full, bwd_flat, (((0,), (0,)), (()...  34.3 us
    psum x1, blocking collectives, shards(): lax.psum(((out_grads[2] + sum_grads[2]).reshape(channels_here), out_grads...  20.8 us
    ppermute x3, starting transfers between devices, assign_streams(): y.append(jax.lax.ppermute(y[-1], chip_axis, perm=entries))  12.6 us
    unnamed x104, local copies, waits for them, and re-layouts  12.4 us
    ppermute x4, waiting for transfers between devices, assign_streams(): v_now.append(jax.lax.ppermute(v_now[-1], chip_axis, perm=crops))  9.68 us
    ppermute x12, waiting for transfers between devices, shifted(): return lax.ppermute(block, axis, route)  7.62 us
    dot_general x5, matrix products, contract(): return jnp.einsum(spec, left, right, preferred_element_type=jnp.float32)  7.11 us
  transfers between devices with their start and end apart: 21, of which 8 were waited for; matrix products, arithmetic and copies ran while one was open for 12% of the time, Pallas kernels for 0%

profile of v1, /device:TPU:0, one launch (start us, length us, event | category | flops | bytes accessed | tf_op | source)
XLA Modules:
  0.0 210.3 jit_solution(16732169567604903135)
XLA Ops:
  7.2 3.0 %collective-permute-start = (bf16[32,1792]{1,0:T(8,128)(2,1)}, bf16[32,1792]{1,0:T(8,128)(2,1)S(1)}, u32[]{:S(2)}, u32[]{:S(2)}) collective-permute-start(bf16[32,1792]{1,0:T(8,128)(2,1)} %bitcast.230), channel_id=1, source_target_pairs={{0,2},{2,4},{4,6},{6,8},{8,10},{10,12},{12,14},{14,0},{1,3},{3,5},... | collective-permute-start | bytes 344072 | tf_op jit(solution)/shard_map/ppermute | solution.py:125
  10.3 3.1 %collective-permute-start.4 = (bf16[32,1792]{1,0:T(8,128)(2,1)}, bf16[32,1792]{1,0:T(8,128)(2,1)S(1)}, u32[]{:S(2)}, u32[]{:S(2)}) collective-permute-start(bf16[32,1792]{1,0:T(8,128)(2,1)} %bitcast.231), channel_id=1, source_target_pairs={{0,14},{2,0},{4,2},{6,4},{8,6},{10,8},{12,10},{14,12},{1,15},{3,1}... | collective-permute-start | bytes 344072 | tf_op jit(solution)/shard_map/ppermute | solution.py:127
  14.6 1.9 collective-permute-start.8
  16.5 1.3 copy.62
  21.5 1.5 collective-permute-start.1
  23.3 5.7 %collective-permute-done.1 = bf16[32,1792]{1,0:T(8,128)(2,1)S(1)} collective-permute-done((bf16[32,1792]{1,0:T(8,128)(2,1)S(1)}, bf16[32,1792]{1,0:T(8,128)(2,1)S(1)}, u32[]{:S(2)}, u32[]{:S(2)}) %collective-permute-start.1) | collective-permute-done | bytes 114720 | tf_op jit(solution)/shard_map/ppermute | solution.py:125
  29.0 4.8 %collective-permute-start.5 = (bf16[32,1792]{1,0:T(8,128)(2,1)S(1)}, bf16[32,1792]{1,0:T(8,128)(2,1)S(1)}, u32[]{:S(2)}, u32[]{:S(2)}) collective-permute-start(bf16[32,1792]{1,0:T(8,128)(2,1)S(1)} %collective-permute-done.4), channel_id=1, source_target_pairs={{0,14},{2,0},{4,2},{6,4},{8,6},{10,8},{12,10},{14,12},{1,15},{3,1}... | collective-permute-start | bytes 344072 | tf_op jit(solution)/shard_map/ppermute | solution.py:127
  33.8 2.7 %collective-permute-done.2 = bf16[32,1792]{1,0:T(8,128)(2,1)S(1)} collective-permute-done((bf16[32,1792]{1,0:T(8,128)(2,1)S(1)}, bf16[32,1792]{1,0:T(8,128)(2,1)S(1)}, u32[]{:S(2)}, u32[]{:S(2)}) %collective-permute-start.2) | collective-permute-done | bytes 114720 | tf_op jit(solution)/shard_map/ppermute | solution.py:125
  38.0 4.8 %collective-permute-start.6 = (bf16[32,1792]{1,0:T(8,128)(2,1)S(1)}, bf16[32,1792]{1,0:T(8,128)(2,1)S(1)}, u32[]{:S(2)}, u32[]{:S(2)}) collective-permute-start(bf16[32,1792]{1,0:T(8,128)(2,1)S(1)} %collective-permute-done.5), channel_id=1, source_target_pairs={{0,14},{2,0},{4,2},{6,4},{8,6},{10,8},{12,10},{14,12},{1,15},{3,1}... | collective-permute-start | bytes 344072 | tf_op jit(solution)/shard_map/ppermute | solution.py:127
  54.5 2.2 %fusion.23 = bf16[128,256]{0,1:T(8,128)(2,1)} fusion(bf16[512,1792]{1,0:T(8,128)(2,1)} %constant_dynamic-update-slice_fusion, s32[]{:T(128)S(6)} %select_n.44, bf16[1,128,1792]{2,1,0:T(8,128)(2,1)S(1)} %copy-done), kind=kOutput, calls=%fused_computation.40 | convolution fusion | flops 117473280 | bytes 1441796 | tf_op jit(solution)/shard_map/dot_general | solution.py:133
  56.8 5.9 %reduce-scatter.3.cloned.1.call-done = bf16[128,128]{0,1:T(8,128)(2,1)} async-done(((bf16[128,256]{0,1:T(8,128)(2,1)}), bf16[128,128]{0,1:T(8,128)(2,1)}) %reduce-scatter.3.cloned.1.call-update) | async-done | bytes 32784 | tf_op jit(solution)/shard_map/reduce_scatter | solution.py:134
  64.9 4.3 %collective-permute-start.7 = (bf16[28,4096]{1,0:T(8,128)(2,1)}, bf16[28,4096]{1,0:T(8,128)(2,1)}, u32[]{:S(2)}, u32[]{:S(2)}) collective-permute-start(bf16[28,4096]{1,0:T(8,128)(2,1)} %convert_element_type.193), channel_id=1, source_target_pairs={{0,2},{2,4},{4,6},{6,8},{8,10},{10,12},{12,14},{1,3},{3,5},{5,7},{... | collective-permute-start | bytes 688136 | tf_op jit(solution)/shard_map/ppermute | solution.py:12
  69.3 1.5 convolution_bitcast_fusion
  70.8 1.5 copy.71
  76.0 5.3 %collective-permute-start.10 = (bf16[28,4096]{1,0:T(8,128)(2,1)S(1)}, bf16[28,4096]{1,0:T(8,128)(2,1)S(1)}, u32[]{:S(2)}, u32[]{:S(2)}) collective-permute-start(bf16[28,4096]{1,0:T(8,128)(2,1)S(1)} %fusion.57), channel_id=1, source_target_pairs={{0,4},{2,6},{4,8},{6,10},{8,12},{10,14},{1,5},{3,7},{5,9},{7,11},{... | collective-permute-start | bytes 688136 | tf_op jit(solution)/shard_map/ppermute | solution.py:12
  82.6 4.5 %collective-permute-start.9 = (f32[28]{0:T(128)S(1)}, f32[28]{0:T(128)S(1)}, u32[]{:S(2)}, u32[]{:S(2)}) collective-permute-start(f32[28]{0:T(128)S(1)} %exponential_multiply_fusion.1), channel_id=1, source_target_pairs={{0,2},{2,4},{4,6},{6,8},{8,10},{10,12},{12,14},{1,3},{3,5},{5,7},{... | collective-permute-start | bytes 344 | tf_op jit(solution)/shard_map/ppermute | solution.py:12
  88.5 1.9 fusion.42
  92.4 7.8 %collective-permute-start.12 = (bf16[28,4096]{1,0:T(8,128)(2,1)}, bf16[28,4096]{1,0:T(8,128)(2,1)}, u32[]{:S(2)}, u32[]{:S(2)}) collective-permute-start(bf16[28,4096]{1,0:T(8,128)(2,1)} %get-tuple-element.40), channel_id=1, source_target_pairs={{0,8},{2,10},{4,12},{6,14},{1,9},{3,11},{5,13},{7,15},{16,24},{18,... | collective-permute-start | bytes 688136 | tf_op jit(solution)/shard_map/ppermute | solution.py:12
  104.0 3.5 %collective-permute-start.11 = (f32[28]{0:T(128)S(1)}, f32[28]{0:T(128)S(1)}, u32[]{:S(2)}, u32[]{:S(2)}) collective-permute-start(f32[28]{0:T(128)S(1)} %get-tuple-element.42), channel_id=1, source_target_pairs={{0,4},{2,6},{4,8},{6,10},{8,12},{10,14},{1,5},{3,7},{5,9},{7,11},{... | collective-permute-start | bytes 344 | tf_op jit(solution)/shard_map/ppermute | solution.py:12
  109.4 5.4 %collective-permute-done.16 = f32[28]{0:T(128)S(1)} collective-permute-done((f32[28]{0:T(128)S(1)}, f32[28]{0:T(128)S(1)}, u32[]{:S(2)}, u32[]{:S(2)}) %collective-permute-start.16) | collective-permute-done | bytes 144 | tf_op jit(solution)/shard_map/ppermute | solution.py:12
  115.7 3.0 %multiply_reduce_fusion.2 = (f32[28]{0:T(128)}, bf16[28,4096]{1,0:T(8,128)(2,1)S(1)}, f32[28,4096]{1,0:T(8,128)}) fusion(bf16[28,4096]{1,0:T(8,128)(2,1)} %collective-permute-done.17, f32[28]{0:T(128)S(1)} %mul.369, bf16[28,4096]{1,0:T(8,128)(2,1)S(1)} %collective-permute-done.15, f32[28]{0:T(128)} %copy-done.31, ...), kind=kLoop, calls=%fused_computation.80 | loop fusion | flops 1949668 | bytes 2064944 | tf_op jit(solution)/shard_map/reduce_sum | solution.py:183
  118.6 1.4 reshape.211
  121.3 1.7 fusion.88
  125.0 1.9 multiply_reduce_fusion
  127.1 1.5 fusion.103
  129.2 3.4 %fusion.12 = (f32[28,128]{1,0:T(8,128)}, f32[28,128]{1,0:T(8,128)}, f32[28,128]{1,0:T(8,128)S(1)}, bf16[128,128]{1,0:T(8,128)(2,1)S(1)}) fusion(f32[28,128]{1,0:T(8,128)} %copy.63, f32[128,128]{1,0:T(8,128)} %fusion.84, f32[128,128]{1,0:T(8,128)} %get-tuple-element.46, f32[28,128]{1,0:T(8,128)} %bitcast.236, pred[128,128]{1,0:T(8,128)(4,1)} %get-tuple-element.45, ...), kind=kOutput, calls=%fused_computation.19 | convolution fusion | flops 66491904 | bytes 1169408 | tf_op jit(solution)/shard_map/transpose(jvp(hts,shp->thp))/dot_general | solution.py:16
  134.9 2.2 %all_gather.3 = bf16[128,256]{0,1:T(8,128)(2,1)S(1)} all-gather(bf16[128,128]{0,1:T(8,128)(2,1)S(1)} %add_convert_fusion), channel_id=1, replica_groups=mesh['section'=2,'seq'=8,'head'=2] {'head'}, dimensions={1}, use_global_device_ids=true | all-gather | bytes 98304 | tf_op jit(solution)/shard_map/all_gather | solution.py:188
  137.0 1.3 convolution_convert_fusion
  141.3 1.5 fusion.1
  145.9 20.8 %all-reduce.4 = (f32[1,1792]{1,0:T(1,128)}, f32[1,28]{1,0:T(1,128)}, f32[1,28]{1,0:T(1,128)}, f32[1,28]{1,0:T(1,128)}) all-reduce(f32[1,1792]{1,0:T(1,128)S(1)} %broadcast_in_dim.47, f32[1,28]{1,0:T(1,128)S(1)} %get-tuple-element.50, f32[1,28]{1,0:T(1,128)S(1)} %get-tuple-element.49, ...), channel_id=1, replica_groups=mesh['section'=2,'seq'=8,'head'=2] {'seq'}, use_global_device_ids=true, to_apply=%region_11.13 | all-reduce | flops 1876 | bytes 15008 | tf_op jit(solution)/shard_map/psum | solution.py:203
  166.7 34.3 %reduce-scatter.5.cloned.1.call-done = bf16[32,1792]{1,0:T(8,128)(2,1)} async-done(((bf16[256,1792]{1,0:T(8,128)(2,1)}), bf16[32,1792]{1,0:T(8,128)(2,1)}) %reduce-scatter.5.cloned.1.call-update) | async-done | bytes 114704 | tf_op jit(solution)/shard_map/reduce_scatter | solution.py:195
  201.1 1.6 bitcast_convert_fusion
  (188 shorter events, 46.8 us)
Async XLA Ops:
  7.2 15.8 %copy-start.25 = (f32[1,28]{1,0:T(1,128)S(1)}, f32[1,28]{1,0:T(1,128)}, u32[]{:S(2)}) copy-start(f32[1,28]{1,0:T(1,128)} %param.14) | copy-start | bytes 340
  7.2 55.6 %reduce-scatter.3.cloned.1.call-start = ((), (), s32[]{:S(2)}) async-start(), calls=%async_computation.2 | async-start | bytes 98304 | tf_op jit(solution)/shard_map/reduce_scatter | solution.py:134
  7.2 14.2 %collective-permute-start = (bf16[32,1792]{1,0:T(8,128)(2,1)}, bf16[32,1792]{1,0:T(8,128)(2,1)S(1)}, u32[]{:S(2)}, u32[]{:S(2)}) collective-permute-start(bf16[32,1792]{1,0:T(8,128)(2,1)} %bitcast.230), channel_id=1, source_target_pairs={{0,2},{2,4},{4,6},{6,8},{8,10},{10,12},{12,14},{14,0},{1,3},{3,5},... | collective-permute-start | bytes 344072 | tf_op jit(solution)/shard_map/ppermute | solution.py:125
  10.3 18.8 %collective-permute-start.4 = (bf16[32,1792]{1,0:T(8,128)(2,1)}, bf16[32,1792]{1,0:T(8,128)(2,1)S(1)}, u32[]{:S(2)}, u32[]{:S(2)}) collective-permute-start(bf16[32,1792]{1,0:T(8,128)(2,1)} %bitcast.231), channel_id=1, source_target_pairs={{0,14},{2,0},{4,2},{6,4},{8,6},{10,8},{12,10},{14,12},{1,15},{3,1}... | collective-permute-start | bytes 344072 | tf_op jit(solution)/shard_map/ppermute | solution.py:127
  14.6 5.5 %collective-permute-start.8 = (s32[1]{0:T(128)}, s32[1]{0:T(128)}, u32[]{:S(2)}, u32[]{:S(2)}) collective-permute-start(s32[1]{0:T(128)} %bitcast.19), channel_id=1, source_target_pairs={{0,2},{2,4},{4,6},{6,8},{8,10},{10,12},{12,14},{1,3},{3,5},{5,7},{... | collective-permute-start | bytes 20 | tf_op jit(solution)/shard_map/ppermute | solution.py:12
  16.5 30.2 %copy-start.5 = (bf16[1,32,1792]{2,1,0:T(8,128)(2,1)S(1)}, bf16[1,32,1792]{2,1,0:T(8,128)(2,1)}, u32[]{:S(2)}) copy-start(bf16[1,32,1792]{2,1,0:T(8,128)(2,1)} %param.12) | copy-start | bytes 344068
  19.1 18.8 %copy-start.2 = (f32[28,1,128]{0,2,1:T(8,128)}, f32[28,1,128]{0,2,1:T(8,128)S(1)}, u32[]{:S(2)}) copy-start(f32[28,1,128]{0,2,1:T(8,128)S(1)} %copy.83) | copy-start | bytes 43012
  21.4 16.5 %copy-start.35 = (f32[128]{0:T(128)}, f32[128]{0:T(128)S(1)}, u32[]{:S(2)}) copy-start(f32[128]{0:T(128)S(1)} %get-tuple-element.44) | copy-start | bytes 1540
  21.4 31.8 %copy-start.20 = (pred[128]{0:T(512)(128)(4,1)}, pred[128]{0:T(512)(128)(4,1)S(1)}, u32[]{:S(2)}) copy-start(pred[128]{0:T(512)(128)(4,1)S(1)} %get-tuple-element.31) | copy-start | bytes 388
  21.4 31.8 %copy-start.22 = (f32[128]{0:T(128)}, f32[128]{0:T(128)S(1)}, u32[]{:S(2)}) copy-start(f32[128]{0:T(128)S(1)} %get-tuple-element.32) | copy-start | bytes 1540
  21.5 7.5 %collective-permute-start.1 = (bf16[32,1792]{1,0:T(8,128)(2,1)S(1)}, bf16[32,1792]{1,0:T(8,128)(2,1)S(1)}, u32[]{:S(2)}, u32[]{:S(2)}) collective-permute-start(bf16[32,1792]{1,0:T(8,128)(2,1)S(1)} %collective-permute-done), channel_id=1, source_target_pairs={{0,2},{2,4},{4,6},{6,8},{8,10},{10,12},{12,14},{14,0},{1,3},{3,5},... | collective-permute-start | bytes 344072 | tf_op jit(solution)/shard_map/ppermute | solution.py:125
  23.2 30.7 %copy-start.15 = (f32[128,28]{0,1:T(8,128)}, f32[128,28]{0,1:T(8,128)S(1)}, u32[]{:S(2)}) copy-start(f32[128,28]{0,1:T(8,128)S(1)} %get-tuple-element.48) | copy-start | bytes 43012
  29.0 7.5 %collective-permute-start.2 = (bf16[32,1792]{1,0:T(8,128)(2,1)S(1)}, bf16[32,1792]{1,0:T(8,128)(2,1)S(1)}, u32[]{:S(2)}, u32[]{:S(2)}) collective-permute-start(bf16[32,1792]{1,0:T(8,128)(2,1)S(1)} %collective-permute-done.1), channel_id=1, source_target_pairs={{0,2},{2,4},{4,6},{6,8},{8,10},{10,12},{12,14},{14,0},{1,3},{3,5},... | collective-permute-start | bytes 344072 | tf_op jit(solution)/shard_map/ppermute | solution.py:125
  29.0 24.8 %copy-start.27 = (f32[28]{0:T(128)}, f32[28]{0:T(128)S(1)}, u32[]{:S(2)}) copy-start(f32[28]{0:T(128)S(1)} %slice_bitcast_fusion) | copy-start | bytes 340
  29.0 8.9 %collective-permute-start.5 = (bf16[32,1792]{1,0:T(8,128)(2,1)S(1)}, bf16[32,1792]{1,0:T(8,128)(2,1)S(1)}, u32[]{:S(2)}, u32[]{:S(2)}) collective-permute-start(bf16[32,1792]{1,0:T(8,128)(2,1)S(1)} %collective-permute-done.4), channel_id=1, source_target_pairs={{0,14},{2,0},{4,2},{6,4},{8,6},{10,8},{12,10},{14,12},{1,15},{3,1}... | collective-permute-start | bytes 344072 | tf_op jit(solution)/shard_map/ppermute | solution.py:127
  36.5 7.6 %collective-permute-start.3 = (bf16[32,1792]{1,0:T(8,128)(2,1)S(1)}, bf16[32,1792]{1,0:T(8,128)(2,1)S(1)}, u32[]{:S(2)}, u32[]{:S(2)}) collective-permute-start(bf16[32,1792]{1,0:T(8,128)(2,1)S(1)} %collective-permute-done.2), channel_id=1, source_target_pairs={{0,2},{2,4},{4,6},{6,8},{8,10},{10,12},{12,14},{14,0},{1,3},{3,5},... | collective-permute-start | bytes 344072 | tf_op jit(solution)/shard_map/ppermute | solution.py:125
  38.0 16.6 %copy-start = (bf16[1,128,1792]{2,1,0:T(8,128)(2,1)S(1)}, bf16[1,128,1792]{2,1,0:T(8,128)(2,1)}, u32[]{:S(2)}) copy-start(bf16[1,128,1792]{2,1,0:T(8,128)(2,1)} %param.9) | copy-start | bytes 1376260
  38.0 10.6 %collective-permute-start.6 = (bf16[32,1792]{1,0:T(8,128)(2,1)S(1)}, bf16[32,1792]{1,0:T(8,128)(2,1)S(1)}, u32[]{:S(2)}, u32[]{:S(2)}) collective-permute-start(bf16[32,1792]{1,0:T(8,128)(2,1)S(1)} %collective-permute-done.5), channel_id=1, source_target_pairs={{0,14},{2,0},{4,2},{6,4},{8,6},{10,8},{12,10},{14,12},{1,15},{3,1}... | collective-permute-start | bytes 344072 | tf_op jit(solution)/shard_map/ppermute | solution.py:127
  56.8 144.3 %reduce-scatter.5.cloned.1.call-start = ((), (), s32[]{:S(2)}) async-start(), calls=%async_computation.3 | async-start | bytes 1032192 | tf_op jit(solution)/shard_map/reduce_scatter | solution.py:195
  64.9 10.0 %collective-permute-start.7 = (bf16[28,4096]{1,0:T(8,128)(2,1)}, bf16[28,4096]{1,0:T(8,128)(2,1)}, u32[]{:S(2)}, u32[]{:S(2)}) collective-permute-start(bf16[28,4096]{1,0:T(8,128)(2,1)} %convert_element_type.193), channel_id=1, source_target_pairs={{0,2},{2,4},{4,6},{6,8},{8,10},{10,12},{12,14},{1,3},{3,5},{5,7},{... | collective-permute-start | bytes 688136 | tf_op jit(solution)/shard_map/ppermute | solution.py:12
  72.6 15.8 %collective-permute-start.13 = (bf16[28,4096]{1,0:T(8,128)(2,1)S(1)}, bf16[28,4096]{1,0:T(8,128)(2,1)S(1)}, u32[]{:S(2)}, u32[]{:S(2)}) collective-permute-start(bf16[28,4096]{1,0:T(8,128)(2,1)S(1)} %convert_element_type.204), channel_id=1, source_target_pairs={{2,0},{4,2},{6,4},{8,6},{10,8},{12,10},{14,12},{3,1},{5,3},{7,5},{... | collective-permute-start | bytes 688136 | tf_op jit(solution)/shard_map/ppermute | solution.py:12
  76.0 12.5 %collective-permute-start.10 = (bf16[28,4096]{1,0:T(8,128)(2,1)S(1)}, bf16[28,4096]{1,0:T(8,128)(2,1)S(1)}, u32[]{:S(2)}, u32[]{:S(2)}) collective-permute-start(bf16[28,4096]{1,0:T(8,128)(2,1)S(1)} %fusion.57), channel_id=1, source_target_pairs={{0,4},{2,6},{4,8},{6,10},{8,12},{10,14},{1,5},{3,7},{5,9},{7,11},{... | collective-permute-start | bytes 688136 | tf_op jit(solution)/shard_map/ppermute | solution.py:12
  81.3 5.9 %collective-permute-start.14 = (f32[28]{0:T(128)S(1)}, f32[28]{0:T(128)S(1)}, u32[]{:S(2)}, u32[]{:S(2)}) collective-permute-start(f32[28]{0:T(128)S(1)} %exponential_multiply_fusion.1), channel_id=1, source_target_pairs={{2,0},{4,2},{6,4},{8,6},{10,8},{12,10},{14,12},{3,1},{5,3},{7,5},{... | collective-permute-start | bytes 344 | tf_op jit(solution)/shard_map/ppermute | solution.py:12
  82.6 5.8 %collective-permute-start.9 = (f32[28]{0:T(128)S(1)}, f32[28]{0:T(128)S(1)}, u32[]{:S(2)}, u32[]{:S(2)}) collective-permute-start(f32[28]{0:T(128)S(1)} %exponential_multiply_fusion.1), channel_id=1, source_target_pairs={{0,2},{2,4},{4,6},{6,8},{8,10},{10,12},{12,14},{1,3},{3,5},{5,7},{... | collective-permute-start | bytes 344 | tf_op jit(solution)/shard_map/ppermute | solution.py:12
  87.2 27.6 %copy-start.31 = (f32[28]{0:T(128)}, f32[28]{0:T(128)S(1)}, u32[]{:S(2)}) copy-start(f32[28]{0:T(128)S(1)} %collective-permute-done.14) | copy-start | bytes 340
  88.5 21.0 %copy-start.32 = (f32[28]{0:T(128)}, f32[28]{0:T(128)S(1)}, u32[]{:S(2)}) copy-start(f32[28]{0:T(128)S(1)} %collective-permute-done.9) | copy-start | bytes 340
  90.4 9.8 %collective-permute-start.15 = (bf16[28,4096]{1,0:T(8,128)(2,1)S(1)}, bf16[28,4096]{1,0:T(8,128)(2,1)S(1)}, u32[]{:S(2)}, u32[]{:S(2)}) collective-permute-start(bf16[28,4096]{1,0:T(8,128)(2,1)S(1)} %get-tuple-element.41), channel_id=1, source_target_pairs={{4,0},{6,2},{8,4},{10,6},{12,8},{14,10},{5,1},{7,3},{9,5},{11,7},{... | collective-permute-start | bytes 688136 | tf_op jit(solution)/shard_map/ppermute | solution.py:12
  92.4 23.3 %collective-permute-start.12 = (bf16[28,4096]{1,0:T(8,128)(2,1)}, bf16[28,4096]{1,0:T(8,128)(2,1)}, u32[]{:S(2)}, u32[]{:S(2)}) collective-permute-start(bf16[28,4096]{1,0:T(8,128)(2,1)} %get-tuple-element.40), channel_id=1, source_target_pairs={{0,8},{2,10},{4,12},{6,14},{1,9},{3,11},{5,13},{7,15},{16,24},{18,... | collective-permute-start | bytes 688136 | tf_op jit(solution)/shard_map/ppermute | solution.py:12
  101.1 14.5 %collective-permute-start.17 = (bf16[28,4096]{1,0:T(8,128)(2,1)}, bf16[28,4096]{1,0:T(8,128)(2,1)}, u32[]{:S(2)}, u32[]{:S(2)}) collective-permute-start(bf16[28,4096]{1,0:T(8,128)(2,1)} %fusion.46), channel_id=1, source_target_pairs={{8,0},{10,2},{12,4},{14,6},{9,1},{11,3},{13,5},{15,7},{24,16},{26,... | collective-permute-start | bytes 688136 | tf_op jit(solution)/shard_map/ppermute | solution.py:12
  104.0 5.4 %collective-permute-start.11 = (f32[28]{0:T(128)S(1)}, f32[28]{0:T(128)S(1)}, u32[]{:S(2)}, u32[]{:S(2)}) collective-permute-start(f32[28]{0:T(128)S(1)} %get-tuple-element.42), channel_id=1, source_target_pairs={{0,4},{2,6},{4,8},{6,10},{8,12},{10,14},{1,5},{3,7},{5,9},{7,11},{... | collective-permute-start | bytes 344 | tf_op jit(solution)/shard_map/ppermute | solution.py:12
  108.1 6.7 %collective-permute-start.16 = (f32[28]{0:T(128)S(1)}, f32[28]{0:T(128)S(1)}, u32[]{:S(2)}, u32[]{:S(2)}) collective-permute-start(f32[28]{0:T(128)S(1)} %get-tuple-element.43), channel_id=1, source_target_pairs={{4,0},{6,2},{8,4},{10,6},{12,8},{14,10},{5,1},{7,3},{9,5},{11,7},{... | collective-permute-start | bytes 344 | tf_op jit(solution)/shard_map/ppermute | solution.py:12
  142.8 23.9 %collective-permute-start.18 = (bf16[1,128,1792]{2,1,0:T(8,128)(2,1)S(1)}, bf16[1,128,1792]{2,1,0:T(8,128)(2,1)S(1)}, u32[]{:S(2)}, u32[]{:S(2)}) collective-permute-start(bf16[1,128,1792]{2,1,0:T(8,128)(2,1)S(1)} %fusion.1), channel_id=1, source_target_pairs={{16,0},{17,1},{18,2},{19,3},{20,4},{21,5},{22,6},{23,7},{24,8},{25... | collective-permute-start | bytes 1376264 | tf_op jit(solution)/shard_map/ppermute | solution.py:12
  (32 other events, 166.5 us)
Sparse Core Ops, SparseCore 0:
  56.9 5.8 reduce-scatter.2
  138.5 62.4 reduce-scatter.4
